TPU v7x, 512 devices: a whole 4x8x8 slice. The times are simulated.
512 devices in a mesh: sub: 32 (over x_lo, z, core), grp: 16 (over x_hi, y).
Axes of the slice: x: 4 (x_hi: 2, x_lo: 2; x = x_hi * 2 + x_lo), y: 8, z: 8, core: 2. Of those that a mesh axis runs over, the one named last changes fastest.
Arguments:
- deflation: bfloat16 [32, 3, 512, 128, 128], P(None, None, 'sub', 'grp'), may hold values from -10 to 10, as said below
- stiffness: bfloat16 [4, 512, 128, 128], P(None, 'sub', 'grp'), may hold values from 0.02 to 40, as said below
- depths: int32 [512], P(('sub', 'grp')), may hold values from 1 to 128, 49152 in all
Outputs:
- coarse_rows: float32 [32, 16, 32, 96], P('sub')
Inputs may be any that keep to these rules, and one draw needn't show every extreme that they name: `deflation`: entries of order one. `stiffness`: positive coefficients. `depths`: the deepest subdomain has all 128 cells live.
All inputs are finite; a program needn't handle non-finite values. No bound on the sum of `depths` on one device may be relied on, other than what follows from the above.
Results may differ from a plain program's by a relative error of at most 0.0003.
Values may be sent and summed in bfloat16 or wider, within the bound.
No kernel may reach another device: no remote copies, remote signals or barrier semaphores. Data moves between devices by JAX's collectives and lax.ppermute only.
A program may use at most 128 MiB of HBM per device.

v0:
```python
import jax
import jax.numpy as jnp
from jax import lax
from jax.sharding import PartitionSpec as P


def from_behind(x, axis, by):
    length = lax.axis_size(axis)
    pairs = [(i, i + by) for i in range(length) if 0 <= i + by < length]
    return lax.ppermute(x, axis, pairs)


def gram_of(left_side, right_side):
    count = left_side.shape[0]
    return jnp.dot(
        left_side.reshape(count, -1),
        right_side.reshape(count, -1).T,
        preferred_element_type=jnp.float32,
    )


def weighted(weight, values):
    return (weight.astype(jnp.float32) * values.astype(jnp.float32)).astype(jnp.bfloat16)


def differences(values, dim_index):
    widened = values.astype(jnp.float32)
    length = widened.shape[dim_index]
    following = jnp.concatenate(
        [
            lax.slice_in_dim(widened, 1, length, axis=dim_index),
            jnp.zeros_like(lax.slice_in_dim(widened, 0, 1, axis=dim_index)),
        ],
        axis=dim_index,
    )
    return (widened - following).astype(jnp.bfloat16)


def local_terms(live_field, coefficients):
    accumulated = gram_of(live_field, weighted(coefficients[0], live_field))
    for entry in range(3):
        stepped = differences(live_field, entry + 2)
        accumulated = accumulated + gram_of(stepped, weighted(coefficients[entry + 1], stepped))
    return accumulated


def shards(deflation, stiffness, depths):
    cell_count = deflation.shape[2] * deflation.shape[3] * deflation.shape[4]
    normalizer = 1.0 / (24.0 * cell_count)
    live_mask = (lax.iota(jnp.int32, deflation.shape[4]) < depths[0]).astype(jnp.bfloat16)
    live_field = deflation * live_mask
    diagonal_block = local_terms(live_field, stiffness)
    top_x = live_field[:, :, -1]
    bottom_x = live_field[:, :, 0]
    weight_top_x = stiffness[1, -1]
    next_x = from_behind(bottom_x, "sub", -1)
    coupling_x = -gram_of(weighted(weight_top_x, top_x), next_x)
    face_term = gram_of(next_x, weighted(weight_top_x, next_x))
    lower_x = from_behind(face_term, "sub", 1)
    diagonal_block = diagonal_block + lower_x
    bottom_y = live_field[:, :, :, 0]
    weight_top_y = stiffness[2, :, -1]
    next_y = from_behind(bottom_y, "grp", -1)
    weight_low_y = from_behind(weight_top_y, "grp", 1)
    diagonal_block = diagonal_block + gram_of(bottom_y, weighted(weight_low_y, bottom_y))
    coupling_y = -gram_of(weighted(weight_top_y, live_field[:, :, :, -1]), next_y)
    row_block = normalizer * jnp.concatenate([diagonal_block, coupling_x, coupling_y], axis=1)
    return lax.all_gather(row_block[None, None], "grp", axis=1, tiled=True)


def solution(mesh):
    in_specs = (P(None, None, "sub", "grp", None), P(None, "sub", "grp", None), P(("sub", "grp")))
    out_specs = P("sub", None, None, None)
    return jax.shard_map(shards, mesh=mesh, in_specs=in_specs, out_specs=out_specs, check_vma=False)
```

profile of v0, /device:TPU:2, one launch (start us, length us, event | category | flops | bytes accessed | tf_op | source)
XLA Modules:
  0.0 105.4 jit_solution(15280825005196992566)
XLA Ops:
  0.0 0.8 slice.49
  0.8 3.5 %collective-permute-start.2 = (bf16[16,128]{1,0:T(8,128)(2,1)S(1)}, bf16[16,128]{1,0:T(8,128)(2,1)S(1)}, u32[]{:S(2)}, u32[]{:S(2)}) collective-permute-start(bf16[16,128]{1,0:T(8,128)(2,1)S(1)} %get-tuple-element.14), channel_id=1, source_target_pairs={{0,1},{1,2},{2,3},{3,4},{4,5},{5,6},{6,7},{7,8},{8,9},{9,10},{10,1... | collective-permute-start | bytes 12296 | tf_op jit(solution)/shard_map/ppermute | solution.py:10
  4.3 0.8 bitcast_convert_fusion
  5.8 6.2 %multiply_convert_fusion.3 = (bf16[32,3,16,8,128]{4,0,3,1,2:T(8,128)(2,1)S(1)}, bf16[32,3,16,8,128]{4,0,3,1,2:T(8,128)(2,1)S(1)}) fusion(f32[16,8,128]{2,1,0:T(8,128)S(1)} %get-tuple-element.22, bf16[128]{0:T(256)(128)(2,1)S(1)} %compare_convert_fusion, bf16[32,3,16,8,128]{4,3,2,1,0:T(8,128)(2,1)} %param.3), kind=kLoop, calls=%fused_computation.6 | loop fusion | flops 6291456 | bytes 9502976 | tf_op jit(solution)/shard_map/convert_element_type | solution.py:23
  12.0 10.1 %collective-permute-start = (bf16[32,3,8,128]{3,0,2,1:T(8,128)(2,1)S(1)}, bf16[32,3,8,128]{3,0,2,1:T(8,128)(2,1)S(1)}, u32[]{:S(2)}, u32[]{:S(2)}) collective-permute-start(bf16[32,3,8,128]{3,0,2,1:T(8,128)(2,1)S(1)} %slice_bitcast_fusion.4), channel_id=1, source_target_pairs={{16,0},{32,16},{48,32},{64,48},{80,64},{96,80},{112,96},{128,112},... | collective-permute-start | bytes 589832 | tf_op jit(solution)/shard_map/ppermute | solution.py:10
  22.1 1.5 %collective-permute-start.3 = (bf16[32,3,16,128]{3,0,1,2:T(8,128)(2,1)S(1)}, bf16[32,3,16,128]{3,0,1,2:T(8,128)(2,1)S(1)}, u32[]{:S(2)}, u32[]{:S(2)}) collective-permute-start(bf16[32,3,16,128]{3,0,1,2:T(8,128)(2,1)S(1)} %slice_bitcast_fusion.1), channel_id=1, source_target_pairs={{1,0},{2,1},{3,2},{4,3},{5,4},{6,5},{7,6},{8,7},{9,8},{10,9},{11,1... | collective-permute-start | bytes 1179656 | tf_op jit(solution)/shard_map/ppermute | solution.py:10
  23.6 3.2 %slice.53 = f32[32,3,16,7,128]{4,0,3,1,2:T(8,128)} slice(bf16[32,3,16,8,128]{4,0,3,1,2:T(8,128)(2,1)S(1)} %get-tuple-element.12), slice={[0:32], [0:3], [0:16], [1:8], [0:128]} | slice | bytes 11010048 | tf_op jit(solution)/shard_map/slice | solution.py:31
  26.8 3.4 %slice.52 = f32[32,3,15,8,128]{4,0,3,1,2:T(8,128)} slice(bf16[32,3,16,8,128]{4,0,3,1,2:T(8,128)(2,1)S(1)} %get-tuple-element.12), slice={[0:32], [0:3], [1:16], [0:8], [0:128]} | slice | bytes 11796480 | tf_op jit(solution)/shard_map/slice | solution.py:31
  30.1 1.0 slice.54
  31.2 0.9 fusion.12
  32.1 12.0 %multiply_convert_fusion = (bf16[32,3,16,8,128]{4,0,3,1,2:T(8,128)(2,1)}, bf16[32,3,16,8,128]{4,0,3,1,2:T(8,128)(2,1)}, bf16[32,3,16,8,128]{4,0,3,1,2:T(8,128)(2...) fusion(f32[16,8,128]{2,1,0:T(8,128)S(1)} %get-tuple-element.19,, ...), kind=kLoop, calls=%fused_computation | loop fusion | flops 25165824 | bytes 39862272 | tf_op jit(solution)/shard_map/convert_element_type | solution.py:23
  44.1 3.9 %fusion.46 = f32[32,32]{1,0:T(8,128)S(1)} fusion(f32[32,32]{1,0:T(8,128)S(1)} %fusion.12, bf16[32,3,16,8,128]{4,0,3,1,2:T(8,128)(2,1)} %get-tuple-element.15, bf16[32,3,16,8,128]{4,0,3,1,2:T(8,128)(2,1)} %get-tuple-element.16), kind=kOutput, calls=%fused_computation.34 | convolution fusion | flops 100664320 | bytes 6299648 | tf_op jit(solution)/shard_map/dot_general | solution.py:15
  48.1 0.7 copy-done.3
  48.8 1.0 fusion.41
  49.8 0.9 copy-done
  50.7 1.0 copy-done.1
  51.7 1.0 fusion.36
  52.6 0.7 bitcast_convert_fusion.4
  53.5 1.9 %collective-permute-start.1 = (f32[32,32]{1,0:T(8,128)S(1)}, f32[32,32]{1,0:T(8,128)S(1)}, u32[]{:S(2)}, u32[]{:S(2)}) collective-permute-start(f32[32,32]{1,0:T(8,128)S(1)} %convolution_bitcast_fusion.3), channel_id=1, source_target_pairs={{0,16},{16,32},{32,48},{48,64},{64,80},{80,96},{96,112},{112,128},... | collective-permute-start | bytes 12296 | tf_op jit(solution)/shard_map/ppermute | solution.py:10
  55.6 5.1 %collective-permute-done.1 = f32[32,32]{1,0:T(8,128)S(1)} collective-permute-done((f32[32,32]{1,0:T(8,128)S(1)}, f32[32,32]{1,0:T(8,128)S(1)}, u32[]{:S(2)}, u32[]{:S(2)}) %collective-permute-start.1) | collective-permute-done | bytes 4128 | tf_op jit(solution)/shard_map/ppermute | solution.py:10
  60.7 0.2 add_bitcast_fusion
  61.0 0.2 fusion.33
  61.3 43.4 %all_gather.3 = f32[1,16,32,96]{3,2,0,1:T(8,128)S(1)} all-gather(f32[1,1,32,96]{3,2,0,1:T(8,128)S(1)} %fusion.61), channel_id=1, replica_groups=mesh['sub'=32,'grp'=16] {'grp'}, dimensions={1}, use_global_device_ids=true | all-gather | bytes 208896 | tf_op jit(solution)/shard_map/all_gather | solution.py:68
  104.7 0.7 copy.118
  (16 shorter events, 0.5 us)
Async XLA Ops:
  0.8 52.5 %collective-permute-start.2 = (bf16[16,128]{1,0:T(8,128)(2,1)S(1)}, bf16[16,128]{1,0:T(8,128)(2,1)S(1)}, u32[]{:S(2)}, u32[]{:S(2)}) collective-permute-start(bf16[16,128]{1,0:T(8,128)(2,1)S(1)} %get-tuple-element.14), channel_id=1, source_target_pairs={{0,1},{1,2},{2,3},{3,4},{4,5},{5,6},{6,7},{7,8},{8,9},{9,10},{10,1... | collective-permute-start | bytes 12296 | tf_op jit(solution)/shard_map/ppermute | solution.py:10
  12.0 41.4 %collective-permute-start = (bf16[32,3,8,128]{3,0,2,1:T(8,128)(2,1)S(1)}, bf16[32,3,8,128]{3,0,2,1:T(8,128)(2,1)S(1)}, u32[]{:S(2)}, u32[]{:S(2)}) collective-permute-start(bf16[32,3,8,128]{3,0,2,1:T(8,128)(2,1)S(1)} %slice_bitcast_fusion.4), channel_id=1, source_target_pairs={{16,0},{32,16},{48,32},{64,48},{80,64},{96,80},{112,96},{128,112},... | collective-permute-start | bytes 589832 | tf_op jit(solution)/shard_map/ppermute | solution.py:10
  22.1 38.9 %collective-permute-start.3 = (bf16[32,3,16,128]{3,0,1,2:T(8,128)(2,1)S(1)}, bf16[32,3,16,128]{3,0,1,2:T(8,128)(2,1)S(1)}, u32[]{:S(2)}, u32[]{:S(2)}) collective-permute-start(bf16[32,3,16,128]{3,0,1,2:T(8,128)(2,1)S(1)} %slice_bitcast_fusion.1), channel_id=1, source_target_pairs={{1,0},{2,1},{3,2},{4,3},{5,4},{6,5},{7,6},{8,7},{9,8},{10,9},{11,1... | collective-permute-start | bytes 1179656 | tf_op jit(solution)/shard_map/ppermute | solution.py:10
  44.1 4.0 %copy-start.2 = (bf16[32,3,16,8,128]{4,0,3,1,2:T(8,128)(2,1)S(1)}, bf16[32,3,16,8,128]{4,0,3,1,2:T(8,128)(2,1)}, u32[]{:S(2)}) copy-start(bf16[32,3,16,8,128]{4,0,3,1,2:T(8,128)(2,1)} %get-tuple-element.17) | copy-start | bytes 9437188
  44.1 4.7 %copy-start.3 = (bf16[32,3,16,8,128]{4,0,3,1,2:T(8,128)(2,1)S(1)}, bf16[32,3,16,8,128]{4,0,3,1,2:T(8,128)(2,1)}, u32[]{:S(2)}) copy-start(bf16[32,3,16,8,128]{4,0,3,1,2:T(8,128)(2,1)} %get-tuple-element.18) | copy-start | bytes 9437188
  48.8 1.9 %copy-start = (bf16[32,3,16,8,128]{4,0,3,1,2:T(8,128)(2,1)S(1)}, bf16[32,3,16,8,128]{4,0,3,1,2:T(8,128)(2,1)}, u32[]{:S(2)}) copy-start(bf16[32,3,16,8,128]{4,0,3,1,2:T(8,128)(2,1)} %get-tuple-element.5) | copy-start | bytes 9437188
  48.8 2.8 %copy-start.1 = (bf16[32,3,16,8,128]{4,0,3,1,2:T(8,128)(2,1)S(1)}, bf16[32,3,16,8,128]{4,0,3,1,2:T(8,128)(2,1)}, u32[]{:S(2)}) copy-start(bf16[32,3,16,8,128]{4,0,3,1,2:T(8,128)(2,1)} %get-tuple-element.6) | copy-start | bytes 9437188
  53.5 7.2 %collective-permute-start.1 = (f32[32,32]{1,0:T(8,128)S(1)}, f32[32,32]{1,0:T(8,128)S(1)}, u32[]{:S(2)}, u32[]{:S(2)}) collective-permute-start(f32[32,32]{1,0:T(8,128)S(1)} %convolution_bitcast_fusion.3), channel_id=1, source_target_pairs={{0,16},{16,32},{32,48},{48,64},{64,80},{80,96},{96,112},{112,128},... | collective-permute-start | bytes 12296 | tf_op jit(solution)/shard_map/ppermute | solution.py:10
where the time goes:
time: 106 us; the launch traced here: 105 us
  blocking collectives  43.4 us (41%)
  other arithmetic  19.8 us (19%)
  starting transfers between devices  17 us (16%)
  local copies, waits for them, and re-layouts  11.7 us (11%)
  matrix products  7.63 us (7%)
  waiting for transfers between devices  5.07 us (5%)
    all_gather x1, blocking collectives, shards(): return lax.all_gather(row_block[None, None], 'grp', axis=1, tiled=True)  43.4 us
    convert_element_type x2, other arithmetic, weighted(): (weight.astype(jnp.float32) * values.astype(jnp.float32)).astype(jnp.bflo...  18.2 us
    ppermute x4, starting transfers between devices, from_behind(): return lax.ppermute(x, axis, pairs)  17 us
    dot_general x8, matrix products, gram_of(): jnp.dot(left_side.reshape(count, -1), right_side.reshape(count, -1).T, pr...  7.63 us
    slice x3, local copies, waits for them, and re-layouts, differences(): lax.slice_in_dim(widened, 1, length, axis=dim_index)  7.61 us
    ppermute x4, waiting for transfers between devices, from_behind(): return lax.ppermute(x, axis, pairs)  5.07 us
    unnamed x9, local copies, waits for them, and re-layouts  3.33 us
  transfers between devices with their start and end apart: 4, of which 1 were waited for; matrix products, arithmetic and copies ran while one was open for 33% of the time, Pallas kernels for 0%

commit v1 on v0

--- a/solution.py
+++ b/solution.py
@@ -65,7 +65,10 @@
     diagonal_block = diagonal_block + gram_of(bottom_y, weighted(weight_low_y, bottom_y))
     coupling_y = -gram_of(weighted(weight_top_y, live_field[:, :, :, -1]), next_y)
     row_block = normalizer * jnp.concatenate([diagonal_block, coupling_x, coupling_y], axis=1)
-    return lax.all_gather(row_block[None, None], "grp", axis=1, tiled=True)
+    return jnp.concatenate(
+        lax.all_to_all(jnp.stack([row_block[None, None]] * lax.axis_size("grp")), "grp", 0, 0),
+        axis=1,
+    )
 
 
 def solution(mesh):

time: 106 us -> 84.5 us (0.80)
  the two profiles are of different devices: /device:TPU:2 before, /device:TPU:10 now
where the time goes in v1:
time: 84.5 us; the launch traced here: 84.1 us
  blocking collectives  21 us (25%)
  other arithmetic  19.8 us (23%)
  starting transfers between devices  18 us (21%)
  local copies, waits for them, and re-layouts  11.8 us (14%)
  matrix products  7.64 us (9%)
  waiting for transfers between devices  5.07 us (6%)
    all_to_all x1, blocking collectives, shards(): lax.all_to_all(jnp.stack([row_block[None, None]] * lax.axis_size('grp')),...  21 us
    convert_element_type x2, other arithmetic, weighted(): (weight.astype(jnp.float32) * values.astype(jnp.float32)).astype(jnp.bflo...  18.2 us
    ppermute x4, starting transfers between devices, from_behind(): return lax.ppermute(x, axis, pairs)  18 us
    dot_general x8, matrix products, gram_of(): jnp.dot(left_side.reshape(count, -1), right_side.reshape(count, -1).T, pr...  7.64 us
    slice x3, local copies, waits for them, and re-layouts, differences(): lax.slice_in_dim(widened, 1, length, axis=dim_index)  7.61 us
    ppermute x4, waiting for transfers between devices, from_behind(): return lax.ppermute(x, axis, pairs)  5.07 us
    unnamed x9, local copies, waits for them, and re-layouts  3.32 us
  transfers between devices with their start and end apart: 4, of which 1 were waited for; matrix products, arithmetic and copies ran while one was open for 41% of the time, Pallas kernels for 0%

profile of v1, /device:TPU:10, one launch (start us, length us, event | category | flops | bytes accessed | tf_op | source)
XLA Modules:
  0.0 84.1 jit_solution(6211183032656931725)
XLA Ops:
  0.0 0.8 slice.49
  0.8 3.5 %collective-permute-start.2 = (bf16[16,128]{1,0:T(8,128)(2,1)S(1)}, bf16[16,128]{1,0:T(8,128)(2,1)S(1)}, u32[]{:S(2)}, u32[]{:S(2)}) collective-permute-start(bf16[16,128]{1,0:T(8,128)(2,1)S(1)} %get-tuple-element.14), channel_id=1, source_target_pairs={{0,1},{1,2},{2,3},{3,4},{4,5},{5,6},{6,7},{7,8},{8,9},{9,10},{10,1... | collective-permute-start | bytes 12296 | tf_op jit(solution)/shard_map/ppermute | solution.py:10
  4.3 0.8 bitcast_convert_fusion
  5.8 6.2 %multiply_convert_fusion.3 = (bf16[32,3,16,8,128]{4,0,3,1,2:T(8,128)(2,1)S(1)}, bf16[32,3,16,8,128]{4,0,3,1,2:T(8,128)(2,1)S(1)}) fusion(f32[16,8,128]{2,1,0:T(8,128)S(1)} %get-tuple-element.22, bf16[128]{0:T(256)(128)(2,1)S(1)} %compare_convert_fusion, bf16[32,3,16,8,128]{4,3,2,1,0:T(8,128)(2,1)} %param.3), kind=kLoop, calls=%fused_computation.6 | loop fusion | flops 6291456 | bytes 9502976 | tf_op jit(solution)/shard_map/convert_element_type | solution.py:23
  12.0 10.1 %collective-permute-start = (bf16[32,3,8,128]{3,0,2,1:T(8,128)(2,1)S(1)}, bf16[32,3,8,128]{3,0,2,1:T(8,128)(2,1)S(1)}, u32[]{:S(2)}, u32[]{:S(2)}) collective-permute-start(bf16[32,3,8,128]{3,0,2,1:T(8,128)(2,1)S(1)} %slice_bitcast_fusion.4), channel_id=1, source_target_pairs={{16,0},{32,16},{48,32},{64,48},{80,64},{96,80},{112,96},{128,112},... | collective-permute-start | bytes 589832 | tf_op jit(solution)/shard_map/ppermute | solution.py:10
  22.1 2.5 %collective-permute-start.3 = (bf16[32,3,16,128]{3,0,1,2:T(8,128)(2,1)S(1)}, bf16[32,3,16,128]{3,0,1,2:T(8,128)(2,1)S(1)}, u32[]{:S(2)}, u32[]{:S(2)}) collective-permute-start(bf16[32,3,16,128]{3,0,1,2:T(8,128)(2,1)S(1)} %slice_bitcast_fusion.1), channel_id=1, source_target_pairs={{1,0},{2,1},{3,2},{4,3},{5,4},{6,5},{7,6},{8,7},{9,8},{10,9},{11,1... | collective-permute-start | bytes 1179656 | tf_op jit(solution)/shard_map/ppermute | solution.py:10
  24.6 3.2 %slice.53 = f32[32,3,16,7,128]{4,0,3,1,2:T(8,128)} slice(bf16[32,3,16,8,128]{4,0,3,1,2:T(8,128)(2,1)S(1)} %get-tuple-element.12), slice={[0:32], [0:3], [0:16], [1:8], [0:128]} | slice | bytes 11010048 | tf_op jit(solution)/shard_map/slice | solution.py:31
  27.9 3.4 %slice.52 = f32[32,3,15,8,128]{4,0,3,1,2:T(8,128)} slice(bf16[32,3,16,8,128]{4,0,3,1,2:T(8,128)(2,1)S(1)} %get-tuple-element.12), slice={[0:32], [0:3], [1:16], [0:8], [0:128]} | slice | bytes 11796480 | tf_op jit(solution)/shard_map/slice | solution.py:31
  31.2 1.0 %slice.54 = f32[32,3,16,8,127]{4,0,3,1,2:T(8,128)S(1)} slice(bf16[32,3,16,8,128]{4,0,3,1,2:T(8,128)(2,1)S(1)} %get-tuple-element.12), slice={[0:32], [0:3], [0:16], [0:8], [1:128]} | slice | bytes 12484608 | tf_op jit(solution)/shard_map/slice | solution.py:31
  32.3 0.9 %fusion.12 = f32[32,32]{1,0:T(8,128)S(1)} fusion(bf16[32,3,16,8,128]{4,0,3,1,2:T(8,128)(2,1)S(1)} %get-tuple-element.11, bf16[32,3,16,8,128]{4,0,3,1,2:T(8,128)(2,1)S(1)} %get-tuple-element.12), kind=kOutput, calls=%fused_computation.20 | convolution fusion | flops 100663296 | bytes 6295552 | tf_op jit(solution)/shard_map/dot_general | solution.py:15
  33.2 12.0 %multiply_convert_fusion = (bf16[32,3,16,8,128]{4,0,3,1,2:T(8,128)(2,1)}, bf16[32,3,16,8,128]{4,0,3,1,2:T(8,128)(2,1)}, bf16[32,3,16,8,128]{4,0,3,1,2:T(8,128)(2...) fusion(f32[16,8,128]{2,1,0:T(8,128)S(1)} %get-tuple-element.19,, ...), kind=kLoop, calls=%fused_computation | loop fusion | flops 25165824 | bytes 39862272 | tf_op jit(solution)/shard_map/convert_element_type | solution.py:23
  45.2 3.9 %fusion.44 = f32[32,32]{1,0:T(8,128)S(1)} fusion(f32[32,32]{1,0:T(8,128)S(1)} %fusion.12, bf16[32,3,16,8,128]{4,0,3,1,2:T(8,128)(2,1)} %get-tuple-element.15, bf16[32,3,16,8,128]{4,0,3,1,2:T(8,128)(2,1)} %get-tuple-element.16), kind=kOutput, calls=%fused_computation.32 | convolution fusion | flops 100664320 | bytes 6299648 | tf_op jit(solution)/shard_map/dot_general | solution.py:15
  49.2 0.7 copy-done.3
  49.9 1.0 %fusion.39 = f32[32,32]{1,0:T(8,128)S(1)} fusion(f32[32,32]{1,0:T(8,128)S(1)} %fusion.44, bf16[32,3,16,8,128]{4,0,3,1,2:T(8,128)(2,1)S(1)} %copy-done.2, bf16[32,3,16,8,128]{4,0,3,1,2:T(8,128)(2,1)S(1)} %copy-done.3), kind=kOutput, calls=%fused_computation.31 | convolution fusion | flops 100664320 | bytes 6299648 | tf_op jit(solution)/shard_map/dot_general | solution.py:15
  50.9 0.9 %copy-done = bf16[32,3,16,8,128]{4,0,3,1,2:T(8,128)(2,1)S(1)} copy-done((bf16[32,3,16,8,128]{4,0,3,1,2:T(8,128)(2,1)S(1)}, bf16[32,3,16,8,128]{4,0,3,1,2:T(8,128)(2,1)}, u32[]{:S(2)}) %copy-start) | copy-done | bytes 3145752
  51.8 1.0 %copy-done.1 = bf16[32,3,16,8,128]{4,0,3,1,2:T(8,128)(2,1)S(1)} copy-done((bf16[32,3,16,8,128]{4,0,3,1,2:T(8,128)(2,1)S(1)}, bf16[32,3,16,8,128]{4,0,3,1,2:T(8,128)(2,1)}, u32[]{:S(2)}) %copy-start.1) | copy-done | bytes 3145752
  52.7 1.0 %fusion.34 = f32[32,32]{1,0:T(8,128)S(1)} fusion(f32[32,32]{1,0:T(8,128)S(1)} %fusion.39, bf16[32,3,16,8,128]{4,0,3,1,2:T(8,128)(2,1)S(1)} %copy-done, bf16[32,3,16,8,128]{4,0,3,1,2:T(8,128)(2,1)S(1)} %copy-done.1), kind=kOutput, calls=%fused_computation.30 | convolution fusion | flops 100664320 | bytes 6299648 | tf_op jit(solution)/shard_map/dot_general | solution.py:15
  53.7 0.7 bitcast_convert_fusion.4
  54.6 1.9 %collective-permute-start.1 = (f32[32,32]{1,0:T(8,128)S(1)}, f32[32,32]{1,0:T(8,128)S(1)}, u32[]{:S(2)}, u32[]{:S(2)}) collective-permute-start(f32[32,32]{1,0:T(8,128)S(1)} %convolution_bitcast_fusion.3), channel_id=1, source_target_pairs={{0,16},{16,32},{32,48},{48,64},{64,80},{80,96},{96,112},{112,128},... | collective-permute-start | bytes 12296 | tf_op jit(solution)/shard_map/ppermute | solution.py:10
  56.7 5.1 %collective-permute-done.1 = f32[32,32]{1,0:T(8,128)S(1)} collective-permute-done((f32[32,32]{1,0:T(8,128)S(1)}, f32[32,32]{1,0:T(8,128)S(1)}, u32[]{:S(2)}, u32[]{:S(2)}) %collective-permute-start.1) | collective-permute-done | bytes 4128 | tf_op jit(solution)/shard_map/ppermute | solution.py:10
  61.8 0.2 add_add_fusion
  62.0 0.2 fusion.32
  62.4 21.0 %all_to_all.5 = f32[16,1,1,32,96]{4,3,2,1,0:T(8,128)S(1)} all-to-all(f32[16,1,1,32,96]{4,3,2,1,0:T(8,128)S(1)} %stack.3), channel_id=1, replica_groups=mesh['sub'=32,'grp'=16] {'grp'}, dimensions={0} | all-to-all | bytes 393216 | tf_op jit(solution)/shard_map/all_to_all | solution.py:69
  83.4 0.7 copy.116
  (17 shorter events, 0.5 us)
Async XLA Ops:
  0.8 53.6 %collective-permute-start.2 = (bf16[16,128]{1,0:T(8,128)(2,1)S(1)}, bf16[16,128]{1,0:T(8,128)(2,1)S(1)}, u32[]{:S(2)}, u32[]{:S(2)}) collective-permute-start(bf16[16,128]{1,0:T(8,128)(2,1)S(1)} %get-tuple-element.14), channel_id=1, source_target_pairs={{0,1},{1,2},{2,3},{3,4},{4,5},{5,6},{6,7},{7,8},{8,9},{9,10},{10,1... | collective-permute-start | bytes 12296 | tf_op jit(solution)/shard_map/ppermute | solution.py:10
  12.0 42.4 %collective-permute-start = (bf16[32,3,8,128]{3,0,2,1:T(8,128)(2,1)S(1)}, bf16[32,3,8,128]{3,0,2,1:T(8,128)(2,1)S(1)}, u32[]{:S(2)}, u32[]{:S(2)}) collective-permute-start(bf16[32,3,8,128]{3,0,2,1:T(8,128)(2,1)S(1)} %slice_bitcast_fusion.4), channel_id=1, source_target_pairs={{16,0},{32,16},{48,32},{64,48},{80,64},{96,80},{112,96},{128,112},... | collective-permute-start | bytes 589832 | tf_op jit(solution)/shard_map/ppermute | solution.py:10
  22.1 39.9 %collective-permute-start.3 = (bf16[32,3,16,128]{3,0,1,2:T(8,128)(2,1)S(1)}, bf16[32,3,16,128]{3,0,1,2:T(8,128)(2,1)S(1)}, u32[]{:S(2)}, u32[]{:S(2)}) collective-permute-start(bf16[32,3,16,128]{3,0,1,2:T(8,128)(2,1)S(1)} %slice_bitcast_fusion.1), channel_id=1, source_target_pairs={{1,0},{2,1},{3,2},{4,3},{5,4},{6,5},{7,6},{8,7},{9,8},{10,9},{11,1... | collective-permute-start | bytes 1179656 | tf_op jit(solution)/shard_map/ppermute | solution.py:10
  45.2 4.0 %copy-start.2 = (bf16[32,3,16,8,128]{4,0,3,1,2:T(8,128)(2,1)S(1)}, bf16[32,3,16,8,128]{4,0,3,1,2:T(8,128)(2,1)}, u32[]{:S(2)}) copy-start(bf16[32,3,16,8,128]{4,0,3,1,2:T(8,128)(2,1)} %get-tuple-element.17) | copy-start | bytes 9437188
  45.2 4.7 %copy-start.3 = (bf16[32,3,16,8,128]{4,0,3,1,2:T(8,128)(2,1)S(1)}, bf16[32,3,16,8,128]{4,0,3,1,2:T(8,128)(2,1)}, u32[]{:S(2)}) copy-start(bf16[32,3,16,8,128]{4,0,3,1,2:T(8,128)(2,1)} %get-tuple-element.18) | copy-start | bytes 9437188
  49.9 1.9 %copy-start = (bf16[32,3,16,8,128]{4,0,3,1,2:T(8,128)(2,1)S(1)}, bf16[32,3,16,8,128]{4,0,3,1,2:T(8,128)(2,1)}, u32[]{:S(2)}) copy-start(bf16[32,3,16,8,128]{4,0,3,1,2:T(8,128)(2,1)} %get-tuple-element.5) | copy-start | bytes 9437188
  49.9 2.8 %copy-start.1 = (bf16[32,3,16,8,128]{4,0,3,1,2:T(8,128)(2,1)S(1)}, bf16[32,3,16,8,128]{4,0,3,1,2:T(8,128)(2,1)}, u32[]{:S(2)}) copy-start(bf16[32,3,16,8,128]{4,0,3,1,2:T(8,128)(2,1)} %get-tuple-element.6) | copy-start | bytes 9437188
  54.6 7.2 %collective-permute-start.1 = (f32[32,32]{1,0:T(8,128)S(1)}, f32[32,32]{1,0:T(8,128)S(1)}, u32[]{:S(2)}, u32[]{:S(2)}) collective-permute-start(f32[32,32]{1,0:T(8,128)S(1)} %convolution_bitcast_fusion.3), channel_id=1, source_target_pairs={{0,16},{16,32},{32,48},{48,64},{64,80},{80,96},{96,112},{112,128},... | collective-permute-start | bytes 12296 | tf_op jit(solution)/shard_map/ppermute | solution.py:10
